TPU v7x, 256 devices: a whole 4x4x8 slice. The times are simulated.
256 devices in a mesh: cfg: 2 (over z_lo), seq: 16 (over z_hi, x), wblk: 8 (over y, core).
Axes of the slice: x: 4, y: 4, z: 8 (z_hi: 4, z_lo: 2; z = z_hi * 2 + z_lo), core: 2. Of those that a mesh axis runs over, the one named last changes fastest.
Arguments:
- text_tokens: bfloat16 [2, 2, 512, 3072], P('cfg', None, 'seq', 'wblk'), may hold values from -16 to 16
- image_tokens: bfloat16 [2, 4096, 3072], P(None, 'seq', 'wblk'), may hold values from -16 to 16
- pooled_vector: float32 [2, 3072], P('cfg', 'seq'), may hold values from -6 to 6
- mod_weight: bfloat16 [3072, 3, 3072], P('seq', None, 'wblk'), may hold values from -0.109375 to 0.109375
- qkv_weight: bfloat16 [3072, 3, 16, 128], P('seq', None, 'wblk'), may hold values from -0.109375 to 0.109375
- up_weight: bfloat16 [3072, 6144], P('seq', 'wblk'), may hold values from -0.109375 to 0.109375
- query_gain: float32 [128], replicated, may hold values from 0.6 to 10
- key_gain: float32 [128], replicated, may hold values from 0.6 to 10
- attn_weight: bfloat16 [2048, 3072], P('wblk', 'seq'), may hold values from -0.125 to 0.125
- down_weight: bfloat16 [6144, 3072], P('wblk', 'seq'), may hold values from -0.078125 to 0.078125
- lengths: int32 [2], replicated, may hold values from 1 to 512, as said below
- timestep: int32 [1], replicated, may hold values from 0 to 27
Outputs:
- text_out: bfloat16 [2, 2, 512, 3072], P('cfg', None, 'seq', 'wblk')
- velocity: float32 [2, 4096, 3072], P('cfg', 'seq', 'wblk')
- new_image: float32 [2, 4096, 3072], P('cfg', 'seq', 'wblk')
Inputs may be any that keep to these rules, and one draw needn't show every extreme that they name: `lengths`: some prompt has all 512 text tokens live in every draw.
All inputs are finite; a program needn't handle non-finite values.
Results may differ from a plain program's by a relative error of at most 0.025.
Values may be sent and summed in bfloat16 or wider, within the bound.
No kernel may reach another device: no remote copies, remote signals or barrier semaphores. Data moves between devices by JAX's collectives and lax.ppermute only.
A program may use at most 128 MiB of HBM per device.

v0:
```python
import math
import jax
import jax.numpy as jnp
from jax import lax
from jax.sharding import PartitionSpec as P

D = 3072
HD = 128
GRID = 64
STEPS = 28
epsilon = 1e-06
guidance = 3.5
time_shift = 3.0
rope_theta = 10000.0


def plan(timestep):
    step_index = timestep[0].astype(jnp.float32)
    time_now = 1.0 - step_index / STEPS
    time_next = 1.0 - (step_index + 1.0) / STEPS
    sigma_now = time_shift * time_now / (1.0 + (time_shift - 1.0) * time_now)
    sigma_next = time_shift * time_next / (1.0 + (time_shift - 1.0) * time_next)
    return (sigma_now, sigma_next - sigma_now)


def time_embedding(sigma_now, dim_count):
    halfwidth = dim_count // 2
    frequency = jnp.exp(-math.log(10000.0) * jnp.arange(halfwidth, dtype=jnp.float32) / halfwidth)
    angles = 1000.0 * sigma_now * frequency
    return jnp.concatenate([jnp.cos(angles), jnp.sin(angles)])


def inverse_freq(dim_count):
    return rope_theta ** (-jnp.arange(0, dim_count, 2, dtype=jnp.float32) / dim_count)


def rotary_angles(height_pos, width_pos):
    still_dims = HD // 8
    axis_dims = (HD - still_dims) // 2
    return jnp.concatenate(
        [
            jnp.zeros((height_pos.shape[0], still_dims // 2), jnp.float32),
            height_pos[:, None] * inverse_freq(axis_dims)[None],
            width_pos[:, None] * inverse_freq(axis_dims)[None],
        ],
        axis=1,
    )


def rotate(vectors, angles):
    paired_dims = vectors.reshape(vectors.shape[:-1] + (HD // 2, 2))
    cosine_table = jnp.cos(angles)[:, None, :]
    sine_table = jnp.sin(angles)[:, None, :]
    first_part = paired_dims[..., 0]
    second_part = paired_dims[..., 1]
    turned = jnp.stack(
        [
            first_part * cosine_table - second_part * sine_table,
            first_part * sine_table + second_part * cosine_table,
        ],
        axis=-1,
    )
    return turned.reshape(vectors.shape)


def head_norm(vectors, gain_vector):
    return (
        vectors
        * lax.rsqrt(jnp.mean(vectors * vectors, axis=-1, keepdims=True) + epsilon)
        * gain_vector
    )


def input_folder(source, pieces):
    width_rows = pieces[0].shape[0]
    first_total = jnp.dot(
        source, pieces[0].reshape(width_rows, -1), preferred_element_type=jnp.float32
    )
    second_total = jnp.dot(source, pieces[1], preferred_element_type=jnp.float32)
    return (first_total, second_total)


def output_folder(attended, activated, pieces):
    block_cols = jnp.dot(attended, pieces[0], preferred_element_type=jnp.float32)
    block_cols = block_cols + jnp.dot(activated, pieces[1], preferred_element_type=jnp.float32)
    return block_cols


def shards(
    text_tokens,
    image_tokens,
    pooled_vector,
    mod_weight,
    qkv_weight,
    up_weight,
    query_gain,
    key_gain,
    attn_weight,
    down_weight,
    lengths,
    timestep,
):
    seq_pos = lax.axis_index("seq")
    cfg_pos = lax.axis_index("cfg")
    prompts = image_tokens.shape[0]
    image_rows = image_tokens.shape[1]
    text_rows = text_tokens.shape[2]
    local_len = text_rows + image_rows
    dim_local = image_tokens.shape[2]
    dim_seq = pooled_vector.shape[1]
    heads_local = qkv_weight.shape[2]
    row_count = prompts * local_len
    sigma_now, step_size = plan(timestep)
    embedded = lax.dynamic_slice_in_dim(time_embedding(sigma_now, D), seq_pos * dim_seq, dim_seq)
    cond_vec = jax.nn.silu(pooled_vector[0] + embedded).astype(jnp.bfloat16)[None]
    mod_terms = jnp.dot(
        cond_vec, mod_weight.reshape(dim_seq, 3 * dim_local), preferred_element_type=jnp.float32
    )
    seq_count = lax.psum(1, "seq")
    mod_spread = jnp.broadcast_to(mod_terms.reshape(1, 3, dim_local), (seq_count, 3, dim_local))
    modulation = jnp.sum(lax.all_to_all(mod_spread, "seq", 0, 0, tiled=True), axis=0)
    local_rows = jnp.concatenate([text_tokens[0], image_tokens], axis=1)
    hidden = local_rows.astype(jnp.float32)
    totals, squares = lax.psum(
        (jnp.sum(hidden, axis=-1), jnp.sum(hidden * hidden, axis=-1)), "wblk"
    )
    average = (totals / D)[..., None]
    variance = (squares / D)[..., None] - average * average
    normed = (
        (hidden - average) * lax.rsqrt(variance + epsilon) * (1.0 + modulation[1]) + modulation[0]
    ).astype(jnp.bfloat16)
    width_rows = qkv_weight.shape[0]
    qkv_cols = 3 * heads_local * HD
    qkv_full = lax.all_gather(qkv_weight.reshape(width_rows, qkv_cols), "seq", axis=0, tiled=True)
    wblk_count = lax.psum(1, "wblk")
    spread = jnp.broadcast_to(
        normed.reshape(row_count, 1, dim_local), (row_count, wblk_count, dim_local)
    )
    gathered = lax.all_to_all(spread, "wblk", 1, 1, tiled=True).reshape(row_count, D)
    up_cols = up_weight.shape[1]
    tail_source = jnp.concatenate(
        [up_weight, jnp.concatenate([attn_weight, down_weight], axis=0).T], axis=1
    )
    tail_source, gathered = lax.optimization_barrier((tail_source, gathered))
    tail_full = lax.all_gather(tail_source, "seq", axis=0, tiled=True)
    up_full, out_weight_t = lax.optimization_barrier(
        (tail_full[:, :up_cols], tail_full[:, up_cols:])
    )
    projected = jnp.einsum("rk,kn->rn", gathered, qkv_full, preferred_element_type=jnp.float32)
    mlp_units = jnp.einsum("rk,kn->rn", gathered, up_full, preferred_element_type=jnp.float32)
    projected = projected.reshape(prompts, local_len, 3, heads_local, HD)
    image_index = seq_pos * image_rows + jnp.arange(image_rows, dtype=jnp.int32)
    height_pos = jnp.concatenate(
        [jnp.zeros((text_rows,), jnp.float32), (image_index // GRID).astype(jnp.float32)]
    )
    width_pos = jnp.concatenate(
        [jnp.zeros((text_rows,), jnp.float32), (image_index % GRID).astype(jnp.float32)]
    )
    angles = rotary_angles(height_pos, width_pos)
    queries = rotate(head_norm(projected[:, :, 0], query_gain), angles).astype(jnp.bfloat16)
    key_rows = rotate(head_norm(projected[:, :, 1], key_gain), angles).astype(jnp.bfloat16)
    values = projected[:, :, 2].astype(jnp.bfloat16)
    scale_factor = HD ** (-0.5)
    pair_count = prompts * heads_local
    subs = seq_count // pair_count
    sub_rows = local_len // subs
    pair_keys = key_rows.transpose(0, 2, 1, 3).reshape(pair_count, local_len, HD)
    pair_values = values.transpose(0, 2, 1, 3).reshape(pair_count, local_len, HD)
    pair_queries = queries.transpose(0, 2, 1, 3).reshape(seq_count, sub_rows, HD)
    send = jnp.concatenate(
        [
            jnp.broadcast_to(pair_keys[:, None], (pair_count, subs, local_len, HD)).reshape(
                seq_count, local_len, HD
            ),
            jnp.broadcast_to(pair_values[:, None], (pair_count, subs, local_len, HD)).reshape(
                seq_count, local_len, HD
            ),
            pair_queries,
        ],
        axis=1,
    )
    received = lax.all_to_all(send, "seq", 0, 0, tiled=True)
    key_piece = received[:, :local_len].reshape(seq_count * local_len, HD)
    value_piece = received[:, local_len : 2 * local_len].reshape(seq_count * local_len, HD)
    query_piece = received[:, 2 * local_len :].reshape(seq_count * sub_rows, HD)
    my_prompt = seq_pos // subs // heads_local
    width_keys = key_piece.shape[0]
    where_global = jnp.arange(width_keys, dtype=jnp.int32)
    shard_index = where_global // local_len
    within = where_global % local_len
    text_index = shard_index * text_rows + within
    key_live = (within >= text_rows) | (text_index < lengths[my_prompt])
    scores = jnp.dot(query_piece, key_piece.T, preferred_element_type=jnp.float32) * scale_factor
    scores = jnp.where(key_live[None, :], scores, -1e30)
    top_score = jnp.max(scores, axis=-1, keepdims=True)
    weights = jnp.exp(scores - top_score)
    denominator = jnp.sum(weights, axis=-1, keepdims=True)
    numerator = jnp.dot(
        weights.astype(jnp.bfloat16), value_piece, preferred_element_type=jnp.float32
    )
    mixed = (numerator / denominator).astype(jnp.bfloat16).reshape(seq_count, sub_rows, HD)
    returned = lax.all_to_all(mixed, "seq", 0, 0, tiled=True)
    attended = returned.reshape(prompts, heads_local, local_len, HD)
    attended = attended.transpose(0, 2, 1, 3).reshape(row_count, heads_local * HD)
    activated = jax.nn.gelu(mlp_units, approximate=True).astype(jnp.bfloat16)
    block_terms = jnp.einsum(
        "bjk,rk->brj",
        out_weight_t.reshape(wblk_count, dim_local, -1),
        jnp.concatenate([attended, activated], axis=1),
        preferred_element_type=jnp.float32,
    )
    branch = lax.psum_scatter(
        block_terms.astype(jnp.bfloat16), "wblk", scatter_dimension=0, tiled=True
    )
    branch = branch.reshape(prompts, local_len, dim_local).astype(jnp.float32)
    layer_out = hidden + modulation[2] * branch
    text_out = layer_out[:, :text_rows].astype(jnp.bfloat16)[None]
    image_out = layer_out[:, text_rows:]
    own_prompts = prompts // 2
    rounded_out = image_out.astype(jnp.bfloat16)
    kept = lax.dynamic_slice_in_dim(rounded_out, cfg_pos * own_prompts, own_prompts, 0)
    given = lax.dynamic_slice_in_dim(rounded_out, (1 - cfg_pos) * own_prompts, own_prompts, 0)
    taken = lax.ppermute(given, "cfg", [(0, 1), (1, 0)]).astype(jnp.float32)
    kept = kept.astype(jnp.float32)
    conditional = jnp.where(cfg_pos == 0, kept, taken)
    unconditional = jnp.where(cfg_pos == 0, taken, kept)
    velocity = unconditional + guidance * (conditional - unconditional)
    latent = lax.dynamic_slice_in_dim(image_tokens, cfg_pos * own_prompts, own_prompts, 0).astype(
        jnp.float32
    )
    new_image = latent + step_size * velocity
    return (text_out, velocity, new_image)


def solution(mesh):
    in_specs = (
        P("cfg", None, "seq", "wblk"),
        P(None, "seq", "wblk"),
        P("cfg", "seq"),
        P("seq", None, "wblk"),
        P("seq", None, "wblk", None),
        P("seq", "wblk"),
        P(),
        P(),
        P("wblk", "seq"),
        P("wblk", "seq"),
        P(),
        P(),
    )
    out_specs = (P("cfg", None, "seq", "wblk"), P("cfg", "seq", "wblk"), P("cfg", "seq", "wblk"))
    return jax.shard_map(shards, mesh=mesh, in_specs=in_specs, out_specs=out_specs, check_vma=False)
```

profile of v0, /device:TPU:2, one launch (start us, length us, event | category | flops | bytes accessed | tf_op | source)
XLA Modules:
  0.0 356.4 jit_solution(5952095517683835310)
XLA Ops:
  7.2 1.9 reshape.270
  11.6 11.5 %all-to-all-start = ((f32[16,3,384]{2,1,0:T(4,128)}), f32[16,3,384]{2,1,0:T(4,128)S(1)}, u32[]{:S(2)}, u32[]{:S(2)}) async-start(f32[16,3,384]{2,1,0:T(4,128)} %broadcast_in_dim.24), calls=%async_computation | async-start | bytes 196608 | tf_op jit(solution)/shard_map/all_to_all | solution.py:121
  24.3 14.8 %all-reduce.2 = (f32[2,288]{1,0:T(2,128)S(1)}, f32[2,288]{1,0:T(2,128)S(1)}) all-reduce(f32[2,288]{1,0:T(2,128)S(1)} %get-tuple-element.12, f32[2,288]{1,0:T(2,128)S(1)} %get-tuple-element.11), channel_id=1, replica_groups=mesh['cfg'=2,'seq'=16,'wblk'=8] {'wblk'}, use_global_device_ids=true, to_apply=%region_4.5 | all-reduce | flops 1152 | bytes 9216 | tf_op jit(solution)/shard_map/psum | solution.py:124
  40.5 2.1 broadcast_in_dim.26
  42.6 4.6 %all-to-all-start.1 = ((bf16[576,8,384]{2,0,1:T(8,128)(2,1)}), bf16[576,8,384]{2,0,1:T(8,128)(2,1)}, u32[]{:S(2)}, u32[]{:S(2)}) async-start(bf16[576,8,384]{2,0,1:T(8,128)(2,1)} %broadcast_in_dim.26), calls=%async_computation.1 | async-start | bytes 7077888 | tf_op jit(solution)/shard_map/all_to_all | solution.py:139
  48.3 41.6 %all-to-all-done.1 = bf16[576,8,384]{2,0,1:T(8,128)(2,1)} async-done(((bf16[576,8,384]{2,0,1:T(8,128)(2,1)}), bf16[576,8,384]{2,0,1:T(8,128)(2,1)}, u32[]{:S(2)}, u32[]{:S(2)}) %all-to-all-start.1) | async-done | bytes 3538976 | tf_op jit(solution)/shard_map/all_to_all | solution.py:139
  89.9 4.4 %copy.66 = bf16[8,72,8,384]{3,2,0,1:T(8,128)(2,1)} copy(bf16[8,72,8,384]{3,2,1,0:T(8,128)(2,1)} %bitcast.42) | data formatting | bytes 7077888 | tf_op jit(solution)/shard_map/reshape | solution.py:139
  95.3 7.6 %fusion.60 = f32[576,768]{1,0:T(8,128)} fusion(bf16[576,3072]{1,0:T(8,128)(2,1)} %bitcast.91, bf16[3072,768]{1,0:T(8,128)(2,1)} %all-gather.3.cloned.1.call-done), kind=kOutput, calls=%fused_computation.113 | convolution fusion | flops 2717908992 | bytes 10027008 | tf_op jit(solution)/shard_map/rk,kn->rn/dot_general | solution.py:149
  102.9 2.2 reshape.271
  113.3 1.7 pad_maximum_fusion
  115.0 10.0 %all-to-all-start.2 = ((bf16[16,648,128]{2,1,0:T(8,128)(2,1)}), bf16[16,648,128]{2,1,0:T(8,128)(2,1)S(1)}, u32[]{:S(2)}, u32[]{:S(2)}) async-start(bf16[16,648,128]{2,1,0:T(8,128)(2,1)} %pad_maximum_fusion), calls=%async_computation.2 | async-start | bytes 5308416 | tf_op jit(solution)/shard_map/all_to_all | solution.py:182
  126.5 82.2 %all-to-all-done.2 = bf16[16,648,128]{2,1,0:T(8,128)(2,1)S(1)} async-done(((bf16[16,648,128]{2,1,0:T(8,128)(2,1)}), bf16[16,648,128]{2,1,0:T(8,128)(2,1)S(1)}, u32[]{:S(2)}, u32[]{:S(2)}) %all-to-all-start.2) | async-done | bytes 2654240 | tf_op jit(solution)/shard_map/all_to_all | solution.py:182
  208.9 3.5 fusion.59
  212.4 4.2 %fusion.1 = f32[1152]{0:T(1024)S(1)} fusion(f32[1152,4608]{1,0:T(8,128)S(1)} %get-tuple-element.37, f32[1152]{0:T(1024)S(1)} %get-tuple-element.36), kind=kLoop, calls=%fused_computation.3 | loop fusion | flops 10615680 | bytes 21242880 | tf_op jit(solution)/shard_map/reduce_sum | solution.py:197
  216.6 3.2 copy-done.2
  219.9 10.6 %fusion.9 = bf16[1152,128]{1,0:T(8,128)(2,1)S(1)} fusion(bf16[4608,128]{1,0:T(8,128)(2,1)S(1)} %bitcast.87, f32[1152,4608]{1,0:T(8,128)} %copy-done.2, f32[1152]{0:T(1024)S(1)} %get-tuple-element.36, f32[1152]{0:T(1024)S(1)} %fusion.1), kind=kOutput, calls=%fused_computation.11 | convolution fusion | flops 1369866240 | bytes 22717440 | tf_op jit(solution)/shard_map/dot_general | solution.py:198
  230.4 28.2 %all_to_all.20 = bf16[16,72,128]{2,1,0:T(8,128)(2,1)S(1)} all-to-all(bf16[16,72,128]{2,1,0:T(8,128)(2,1)S(1)} %bitcast.94), channel_id=1, replica_groups=mesh['cfg'=2,'seq'=16,'wblk'=8] {'seq'}, dimensions={0} | all-to-all | bytes 589824 | tf_op jit(solution)/shard_map/all_to_all | solution.py:202
  258.9 31.0 %all-gather.5.cloned.1.call-done = bf16[3072,1792]{1,0:T(8,128)(2,1)} async-done(((bf16[192,1792]{1,0:T(8,128)(2,1)}), bf16[3072,1792]{1,0:T(8,128)(2,1)}) %all-gather.5.cloned.1.call-update) | async-done | bytes 11010064 | tf_op jit(solution)/shard_map/all_gather | solution.py:145
  289.8 2.3 slice-done.1
  293.3 3.1 fusion.19
  296.4 5.4 %convert_bitcast_fusion = bf16[8,576,384]{2,1,0:T(8,128)(2,1)} fusion(bf16[8,384,1024]{2,1,0:T(8,128)(2,1)S(1)} %bitcast.84, bf16[576,768]{1,0:T(8,128)(2,1)S(1)} %fusion.19, bf16[576,256]{1,0:T(8,128)(2,1)S(1)} %bitcast.106), kind=kOutput, calls=%fused_computation.7 | convolution fusion | flops 3628007424 | bytes 11010048 | tf_op jit(solution)/shard_map/bjk,rk->brj/dot_general | solution.py:206
  301.9 40.0 %reduce-scatter.2.cloned.1.call-done = bf16[1,576,384]{2,1,0:T(8,128)(2,1)} async-done(((bf16[8,576,384]{2,1,0:T(8,128)(2,1)}), bf16[1,576,384]{2,1,0:T(8,128)(2,1)}) %reduce-scatter.2.cloned.1.call-update) | async-done | bytes 442384 | tf_op jit(solution)/shard_map/reduce_scatter | solution.py:212
  343.1 1.5 collective-permute-start
  345.3 3.6 %collective-permute-done = bf16[1,256,384]{2,1,0:T(8,128)(2,1)S(1)} collective-permute-done((bf16[1,256,384]{2,1,0:T(8,128)(2,1)S(1)}, bf16[1,256,384]{2,1,0:T(8,128)(2,1)S(1)}, u32[]{:S(2)}, u32[]{:S(2)}) %collective-permute-start) | collective-permute-done | bytes 196640 | tf_op jit(solution)/shard_map/ppermute | solution.py:223
  (88 shorter events, 20.3 us)
Async XLA Ops:
  7.2 3.5 copy-start
  7.2 32.2 %copy-start.3 = (bf16[2,256,384]{2,1,0:T(8,128)(2,1)S(1)}, bf16[2,256,384]{2,1,0:T(8,128)(2,1)}, u32[]{:S(2)}) copy-start(bf16[2,256,384]{2,1,0:T(8,128)(2,1)} %param.13) | copy-start | bytes 1179652
  7.2 88.1 %all-gather.3.cloned.1.call-start = ((), (), s32[]{:S(2)}) async-start(), calls=%async_computation.5 | async-start | bytes 5013504 | tf_op jit(solution)/shard_map/all_gather | solution.py:134
  11.6 27.8 %all-to-all-start = ((f32[16,3,384]{2,1,0:T(4,128)}), f32[16,3,384]{2,1,0:T(4,128)S(1)}, u32[]{:S(2)}, u32[]{:S(2)}) async-start(f32[16,3,384]{2,1,0:T(4,128)} %broadcast_in_dim.24), calls=%async_computation | async-start | bytes 196608 | tf_op jit(solution)/shard_map/all_to_all | solution.py:121
  42.6 4.7 %copy-start.6 = (bf16[768,192]{0,1:T(8,128)(2,1)S(1)}, bf16[768,192]{0,1:T(8,128)(2,1)}, u32[]{:S(2)}) copy-start(bf16[768,192]{0,1:T(8,128)(2,1)} %param.21) | copy-start | bytes 884740
  42.6 4.7 %copy-start.8 = (bf16[256,192]{0,1:T(8,128)(2,1)S(1)}, bf16[256,192]{0,1:T(8,128)(2,1)}, u32[]{:S(2)}) copy-start(bf16[256,192]{0,1:T(8,128)(2,1)} %param.20) | copy-start | bytes 294916
  42.6 4.8 %copy-start.7 = (bf16[192,768]{1,0:T(8,128)(2,1)S(1)}, bf16[192,768]{1,0:T(8,128)(2,1)}, u32[]{:S(2)}) copy-start(bf16[192,768]{1,0:T(8,128)(2,1)} %param.17) | copy-start | bytes 884740
  42.6 47.3 %all-to-all-start.1 = ((bf16[576,8,384]{2,0,1:T(8,128)(2,1)}), bf16[576,8,384]{2,0,1:T(8,128)(2,1)}, u32[]{:S(2)}, u32[]{:S(2)}) async-start(bf16[576,8,384]{2,0,1:T(8,128)(2,1)} %broadcast_in_dim.26), calls=%async_computation.1 | async-start | bytes 7077888 | tf_op jit(solution)/shard_map/all_to_all | solution.py:139
  47.2 242.6 %all-gather.5.cloned.1.call-start = ((), (), s32[]{:S(2)}) async-start(), calls=%async_computation.6 | async-start | bytes 11698176 | tf_op jit(solution)/shard_map/all_gather | solution.py:145
  89.9 4.5 %copy-start.9 = (f32[128]{0:T(128)S(1)}, f32[128]{0:T(128)}, u32[]{:S(2)}) copy-start(f32[128]{0:T(128)} %param.18) | copy-start | bytes 1540
  89.9 4.6 %copy-start.10 = (f32[128]{0:T(128)S(1)}, f32[128]{0:T(128)}, u32[]{:S(2)}) copy-start(f32[128]{0:T(128)} %param.19) | copy-start | bytes 1540
  115.0 10.3 %copy-start.11 = (s32[2]{0:T(128)S(1)}, s32[2]{0:T(128)}, u32[]{:S(2)}) copy-start(s32[2]{0:T(128)} %param.22) | copy-start | bytes 28
  115.0 93.7 %all-to-all-start.2 = ((bf16[16,648,128]{2,1,0:T(8,128)(2,1)}), bf16[16,648,128]{2,1,0:T(8,128)(2,1)S(1)}, u32[]{:S(2)}, u32[]{:S(2)}) async-start(bf16[16,648,128]{2,1,0:T(8,128)(2,1)} %pad_maximum_fusion), calls=%async_computation.2 | async-start | bytes 5308416 | tf_op jit(solution)/shard_map/all_to_all | solution.py:182
  125.0 216.9 %reduce-scatter.2.cloned.1.call-start = ((), (), s32[]{:S(2)}) async-start(), calls=%async_computation.7 | async-start | bytes 3981312 | tf_op jit(solution)/shard_map/reduce_scatter | solution.py:212
  212.4 7.5 %copy-start.2 = (f32[1152,4608]{1,0:T(8,128)}, f32[1152,4608]{1,0:T(8,128)S(1)}, u32[]{:S(2)}) copy-start(f32[1152,4608]{1,0:T(8,128)S(1)} %get-tuple-element.37) | copy-start | bytes 63700996
  289.8 2.3 slice-start.1
  289.8 3.5 copy-start.4
  293.3 3.1 slice-start
  301.8 40.1 %copy-start.5 = (bf16[1,2,32,384]{3,2,1,0:T(8,128)(2,1)S(1)}, bf16[1,2,32,384]{3,2,1,0:T(8,128)(2,1)}, u32[]{:S(2)}) copy-start(bf16[1,2,32,384]{3,2,1,0:T(8,128)(2,1)} %param.12) | copy-start | bytes 147460
  301.8 48.1 %copy-start.1 = (bf16[192,3,384]{2,0,1:T(8,128)(2,1)S(1)}, bf16[192,3,384]{2,0,1:T(8,128)(2,1)}, u32[]{:S(2)}) copy-start(bf16[192,3,384]{2,0,1:T(8,128)(2,1)} %param.15) | copy-start | bytes 1327108
  343.1 5.8 %collective-permute-start = (bf16[1,256,384]{2,1,0:T(8,128)(2,1)S(1)}, bf16[1,256,384]{2,1,0:T(8,128)(2,1)S(1)}, u32[]{:S(2)}, u32[]{:S(2)}) collective-permute-start(bf16[1,256,384]{2,1,0:T(8,128)(2,1)S(1)} %constant_dynamic-slice_fusion), channel_id=1, source_target_pairs={{0,128},{128,0},{1,129},{129,1},{2,130},{130,2},{3,131},{131,3},{4... | collective-permute-start | bytes 589832 | tf_op jit(solution)/shard_map/ppermute | solution.py:223
Sparse Core Ops, SparseCore 0:
  11.0 81.1 all-gather.2
  94.6 195.1 all-gather.4
  301.9 39.9 reduce-scatter.1
where the time goes:
time: 357 us; the launch traced here: 356 us
  waiting for transfers between devices  198 us (55%)
  blocking collectives  43 us (12%)
  matrix products  30.3 us (8%)
  starting transfers between devices  28 us (8%)
  local copies, waits for them, and re-layouts  25 us (7%)
  other arithmetic  16.8 us (5%)
  between operations  14.9 us (4%)
    all_to_all x1, waiting for transfers between devices, shards(): received = lax.all_to_all(send, 'seq', 0, 0, tiled=True)  82.2 us
    all_to_all x1, waiting for transfers between devices, shards(): lax.all_to_all(spread, 'wblk', 1, 1, tiled=True).reshape(row_count, D)  41.6 us
    reduce_scatter x1, waiting for transfers between devices, shards(): lax.psum_scatter(block_terms.astype(jnp.bfloat16), 'wblk', scatter_dimens...  40 us
    all_gather x1, waiting for transfers between devices, shards(): tail_full = lax.all_gather(tail_source, 'seq', axis=0, tiled=True)  31 us
    all_to_all x1, blocking collectives, shards(): returned = lax.all_to_all(mixed, 'seq', 0, 0, tiled=True)  28.2 us
    psum x1, blocking collectives, shards(): lax.psum((jnp.sum(hidden, axis=-1), jnp.sum(hidden * hidden, axis=-1)), '...  14.8 us
    all_to_all x1, starting transfers between devices, shards(): lax.all_to_all(mod_spread, 'seq', 0, 0, tiled=True)  11.5 us
    dot_general x1, matrix products, shards(): jnp.dot(weights.astype(jnp.bfloat16), value_piece, preferred_element_type...  10.6 us
  transfers between devices with their start and end apart: 7, of which 5 were waited for; matrix products, arithmetic and copies ran while one was open for 15% of the time, Pallas kernels for 0%

commit v1 on v0

--- a/solution.py
+++ b/solution.py
@@ -3,6 +3,7 @@
 import jax.numpy as jnp
 from jax import lax
 from jax.sharding import PartitionSpec as P
+from jax.lax import all_to_all, axis_size
 
 D = 3072
 HD = 128
@@ -136,7 +137,13 @@
     spread = jnp.broadcast_to(
         normed.reshape(row_count, 1, dim_local), (row_count, wblk_count, dim_local)
     )
-    gathered = lax.all_to_all(spread, "wblk", 1, 1, tiled=True).reshape(row_count, D)
+    tell_the_shapes = lambda own_rows, axis_key, array_axis, pos_dim: jnp.concatenate(
+        all_to_all(
+            jnp.stack(jnp.split(own_rows, axis_size(axis_key), array_axis), 0), axis_key, 0, 0
+        ),
+        pos_dim,
+    )
+    gathered = tell_the_shapes(spread, "wblk", 1, 1).reshape(row_count, D)
     up_cols = up_weight.shape[1]
     tail_source = jnp.concatenate(
         [up_weight, jnp.concatenate([attn_weight, down_weight], axis=0).T], axis=1

time: 357 us -> 357 us (level)
    reshape x1 -> x0, local copies, waits for them, and re-layouts: 4.44 us -> none  [shards(): lax.all_to_all(spread, 'wblk', 1, 1, tiled=True).reshape(row_count, D)]
    unnamed x28 -> x29, local copies, waits for them, and re-layouts: 6.38 us -> 10.8 us
where the time goes in v1:
time: 357 us; the launch traced here: 356 us
  waiting for transfers between devices  198 us (55%)
  blocking collectives  43 us (12%)
  matrix products  30.3 us (8%)
  starting transfers between devices  28 us (8%)
  local copies, waits for them, and re-layouts  25 us (7%)
  other arithmetic  16.8 us (5%)
  between operations  14.9 us (4%)
    all_to_all x1, waiting for transfers between devices, shards(): received = lax.all_to_all(send, 'seq', 0, 0, tiled=True)  82.2 us
    all_to_all x1, waiting for transfers between devices, shards(): all_to_all(jnp.stack(jnp.split(own_rows, axis_size(axis_key), array_axis)...  41.6 us
    reduce_scatter x1, waiting for transfers between devices, shards(): lax.psum_scatter(block_terms.astype(jnp.bfloat16), 'wblk', scatter_dimens...  40 us
    all_gather x1, waiting for transfers between devices, shards(): tail_full = lax.all_gather(tail_source, 'seq', axis=0, tiled=True)  31 us
    all_to_all x1, blocking collectives, shards(): returned = lax.all_to_all(mixed, 'seq', 0, 0, tiled=True)  28.2 us
    psum x1, blocking collectives, shards(): lax.psum((jnp.sum(hidden, axis=-1), jnp.sum(hidden * hidden, axis=-1)), '...  14.8 us
    all_to_all x1, starting transfers between devices, shards(): lax.all_to_all(mod_spread, 'seq', 0, 0, tiled=True)  11.5 us
    unnamed x29, local copies, waits for them, and re-layouts  10.8 us
  transfers between devices with their start and end apart: 7, of which 5 were waited for; matrix products, arithmetic and copies ran while one was open for 15% of the time, Pallas kernels for 0%

profile of v1, /device:TPU:2, one launch (start us, length us, event | category | flops | bytes accessed | tf_op | source)
XLA Modules:
  0.0 356.4 jit_solution(5952095517683835310)
XLA Ops:
  7.2 1.9 reshape.330
  11.6 11.5 %all-to-all-start = ((f32[16,3,384]{2,1,0:T(4,128)}), f32[16,3,384]{2,1,0:T(4,128)S(1)}, u32[]{:S(2)}, u32[]{:S(2)}) async-start(f32[16,3,384]{2,1,0:T(4,128)} %broadcast_in_dim.22), calls=%async_computation | async-start | bytes 196608 | tf_op jit(solution)/shard_map/all_to_all | solution.py:122
  24.3 14.8 %all-reduce.2 = (f32[2,288]{1,0:T(2,128)S(1)}, f32[2,288]{1,0:T(2,128)S(1)}) all-reduce(f32[2,288]{1,0:T(2,128)S(1)} %get-tuple-element.12, f32[2,288]{1,0:T(2,128)S(1)} %get-tuple-element.11), channel_id=1, replica_groups=mesh['cfg'=2,'seq'=16,'wblk'=8] {'wblk'}, use_global_device_ids=true, to_apply=%region_4.5 | all-reduce | flops 1152 | bytes 9216 | tf_op jit(solution)/shard_map/psum | solution.py:125
  40.5 2.1 stack.8
  42.6 4.6 %all-to-all-start.1 = ((bf16[8,576,1,384]{3,1,2,0:T(8,128)(2,1)}), bf16[8,576,1,384]{3,1,2,0:T(8,128)(2,1)}, u32[]{:S(2)}, u32[]{:S(2)}) async-start(bf16[8,576,1,384]{3,1,2,0:T(8,128)(2,1)} %stack.8), calls=%async_computation.1 | async-start | bytes 7077888 | tf_op jit(solution)/shard_map/all_to_all | solution.py:141
  48.3 41.6 %all-to-all-done.1 = bf16[8,576,1,384]{3,1,2,0:T(8,128)(2,1)} async-done(((bf16[8,576,1,384]{3,1,2,0:T(8,128)(2,1)}), bf16[8,576,1,384]{3,1,2,0:T(8,128)(2,1)}, u32[]{:S(2)}, u32[]{:S(2)}) %all-to-all-start.1) | async-done | bytes 3538976 | tf_op jit(solution)/shard_map/all_to_all | solution.py:141
  89.9 4.4 %copy.59 = bf16[72,8,8,384]{3,1,2,0:T(8,128)(2,1)} copy(bf16[72,8,8,384]{3,1,0,2:T(8,128)(2,1)} %bitcast.69) | data formatting | bytes 7077888
  95.3 7.6 %fusion.60 = f32[576,768]{1,0:T(8,128)} fusion(bf16[576,3072]{1,0:T(8,128)(2,1)} %bitcast.96, bf16[3072,768]{1,0:T(8,128)(2,1)} %all-gather.3.cloned.1.call-done), kind=kOutput, calls=%fused_computation.113 | convolution fusion | flops 2717908992 | bytes 10027008 | tf_op jit(solution)/shard_map/rk,kn->rn/dot_general | solution.py:156
  102.9 2.2 reshape.331
  113.3 1.7 pad_maximum_fusion
  115.0 10.0 %all-to-all-start.2 = ((bf16[16,648,128]{2,1,0:T(8,128)(2,1)}), bf16[16,648,128]{2,1,0:T(8,128)(2,1)S(1)}, u32[]{:S(2)}, u32[]{:S(2)}) async-start(bf16[16,648,128]{2,1,0:T(8,128)(2,1)} %pad_maximum_fusion), calls=%async_computation.2 | async-start | bytes 5308416 | tf_op jit(solution)/shard_map/all_to_all | solution.py:189
  126.5 82.2 %all-to-all-done.2 = bf16[16,648,128]{2,1,0:T(8,128)(2,1)S(1)} async-done(((bf16[16,648,128]{2,1,0:T(8,128)(2,1)}), bf16[16,648,128]{2,1,0:T(8,128)(2,1)S(1)}, u32[]{:S(2)}, u32[]{:S(2)}) %all-to-all-start.2) | async-done | bytes 2654240 | tf_op jit(solution)/shard_map/all_to_all | solution.py:189
  208.9 3.5 fusion.59
  212.4 4.2 %fusion.1 = f32[1152]{0:T(1024)S(1)} fusion(f32[1152,4608]{1,0:T(8,128)S(1)} %get-tuple-element.37, f32[1152]{0:T(1024)S(1)} %get-tuple-element.36), kind=kLoop, calls=%fused_computation.3 | loop fusion | flops 10615680 | bytes 21242880 | tf_op jit(solution)/shard_map/reduce_sum | solution.py:204
  216.6 3.2 copy-done.2
  219.9 10.6 %fusion.9 = bf16[1152,128]{1,0:T(8,128)(2,1)S(1)} fusion(bf16[4608,128]{1,0:T(8,128)(2,1)S(1)} %bitcast.92, f32[1152,4608]{1,0:T(8,128)} %copy-done.2, f32[1152]{0:T(1024)S(1)} %get-tuple-element.36, f32[1152]{0:T(1024)S(1)} %fusion.1), kind=kOutput, calls=%fused_computation.11 | convolution fusion | flops 1369866240 | bytes 22717440 | tf_op jit(solution)/shard_map/dot_general | solution.py:205
  230.4 28.2 %all_to_all.20 = bf16[16,72,128]{2,1,0:T(8,128)(2,1)S(1)} all-to-all(bf16[16,72,128]{2,1,0:T(8,128)(2,1)S(1)} %bitcast.99), channel_id=1, replica_groups=mesh['cfg'=2,'seq'=16,'wblk'=8] {'seq'}, dimensions={0} | all-to-all | bytes 589824 | tf_op jit(solution)/shard_map/all_to_all | solution.py:209
  258.9 31.0 %all-gather.5.cloned.1.call-done = bf16[3072,1792]{1,0:T(8,128)(2,1)} async-done(((bf16[192,1792]{1,0:T(8,128)(2,1)}), bf16[3072,1792]{1,0:T(8,128)(2,1)}) %all-gather.5.cloned.1.call-update) | async-done | bytes 11010064 | tf_op jit(solution)/shard_map/all_gather | solution.py:152
  289.8 2.3 slice-done.1
  293.3 3.1 fusion.19
  296.4 5.4 %convert_bitcast_fusion = bf16[8,576,384]{2,1,0:T(8,128)(2,1)} fusion(bf16[8,384,1024]{2,1,0:T(8,128)(2,1)S(1)} %bitcast.89, bf16[576,768]{1,0:T(8,128)(2,1)S(1)} %fusion.19, bf16[576,256]{1,0:T(8,128)(2,1)S(1)} %bitcast.111), kind=kOutput, calls=%fused_computation.7 | convolution fusion | flops 3628007424 | bytes 11010048 | tf_op jit(solution)/shard_map/bjk,rk->brj/dot_general | solution.py:213
  301.9 40.0 %reduce-scatter.2.cloned.1.call-done = bf16[1,576,384]{2,1,0:T(8,128)(2,1)} async-done(((bf16[8,576,384]{2,1,0:T(8,128)(2,1)}), bf16[1,576,384]{2,1,0:T(8,128)(2,1)}) %reduce-scatter.2.cloned.1.call-update) | async-done | bytes 442384 | tf_op jit(solution)/shard_map/reduce_scatter | solution.py:219
  343.1 1.5 collective-permute-start
  345.3 3.6 %collective-permute-done = bf16[1,256,384]{2,1,0:T(8,128)(2,1)S(1)} collective-permute-done((bf16[1,256,384]{2,1,0:T(8,128)(2,1)S(1)}, bf16[1,256,384]{2,1,0:T(8,128)(2,1)S(1)}, u32[]{:S(2)}, u32[]{:S(2)}) %collective-permute-start) | collective-permute-done | bytes 196640 | tf_op jit(solution)/shard_map/ppermute | solution.py:230
  (88 shorter events, 20.3 us)
Async XLA Ops:
  7.2 3.5 copy-start
  7.2 32.2 %copy-start.3 = (bf16[2,256,384]{2,1,0:T(8,128)(2,1)S(1)}, bf16[2,256,384]{2,1,0:T(8,128)(2,1)}, u32[]{:S(2)}) copy-start(bf16[2,256,384]{2,1,0:T(8,128)(2,1)} %param.13) | copy-start | bytes 1179652
  7.2 88.1 %all-gather.3.cloned.1.call-start = ((), (), s32[]{:S(2)}) async-start(), calls=%async_computation.5 | async-start | bytes 5013504 | tf_op jit(solution)/shard_map/all_gather | solution.py:135
  11.6 27.8 %all-to-all-start = ((f32[16,3,384]{2,1,0:T(4,128)}), f32[16,3,384]{2,1,0:T(4,128)S(1)}, u32[]{:S(2)}, u32[]{:S(2)}) async-start(f32[16,3,384]{2,1,0:T(4,128)} %broadcast_in_dim.22), calls=%async_computation | async-start | bytes 196608 | tf_op jit(solution)/shard_map/all_to_all | solution.py:122
  42.6 4.7 %copy-start.6 = (bf16[768,192]{0,1:T(8,128)(2,1)S(1)}, bf16[768,192]{0,1:T(8,128)(2,1)}, u32[]{:S(2)}) copy-start(bf16[768,192]{0,1:T(8,128)(2,1)} %param.21) | copy-start | bytes 884740
  42.6 4.7 %copy-start.8 = (bf16[256,192]{0,1:T(8,128)(2,1)S(1)}, bf16[256,192]{0,1:T(8,128)(2,1)}, u32[]{:S(2)}) copy-start(bf16[256,192]{0,1:T(8,128)(2,1)} %param.20) | copy-start | bytes 294916
  42.6 4.8 %copy-start.7 = (bf16[192,768]{1,0:T(8,128)(2,1)S(1)}, bf16[192,768]{1,0:T(8,128)(2,1)}, u32[]{:S(2)}) copy-start(bf16[192,768]{1,0:T(8,128)(2,1)} %param.17) | copy-start | bytes 884740
  42.6 47.3 %all-to-all-start.1 = ((bf16[8,576,1,384]{3,1,2,0:T(8,128)(2,1)}), bf16[8,576,1,384]{3,1,2,0:T(8,128)(2,1)}, u32[]{:S(2)}, u32[]{:S(2)}) async-start(bf16[8,576,1,384]{3,1,2,0:T(8,128)(2,1)} %stack.8), calls=%async_computation.1 | async-start | bytes 7077888 | tf_op jit(solution)/shard_map/all_to_all | solution.py:141
  47.2 242.6 %all-gather.5.cloned.1.call-start = ((), (), s32[]{:S(2)}) async-start(), calls=%async_computation.6 | async-start | bytes 11698176 | tf_op jit(solution)/shard_map/all_gather | solution.py:152
  89.9 4.5 %copy-start.9 = (f32[128]{0:T(128)S(1)}, f32[128]{0:T(128)}, u32[]{:S(2)}) copy-start(f32[128]{0:T(128)} %param.18) | copy-start | bytes 1540
  89.9 4.6 %copy-start.10 = (f32[128]{0:T(128)S(1)}, f32[128]{0:T(128)}, u32[]{:S(2)}) copy-start(f32[128]{0:T(128)} %param.19) | copy-start | bytes 1540
  115.0 10.3 %copy-start.11 = (s32[2]{0:T(128)S(1)}, s32[2]{0:T(128)}, u32[]{:S(2)}) copy-start(s32[2]{0:T(128)} %param.22) | copy-start | bytes 28
  115.0 93.7 %all-to-all-start.2 = ((bf16[16,648,128]{2,1,0:T(8,128)(2,1)}), bf16[16,648,128]{2,1,0:T(8,128)(2,1)S(1)}, u32[]{:S(2)}, u32[]{:S(2)}) async-start(bf16[16,648,128]{2,1,0:T(8,128)(2,1)} %pad_maximum_fusion), calls=%async_computation.2 | async-start | bytes 5308416 | tf_op jit(solution)/shard_map/all_to_all | solution.py:189
  125.0 216.9 %reduce-scatter.2.cloned.1.call-start = ((), (), s32[]{:S(2)}) async-start(), calls=%async_computation.7 | async-start | bytes 3981312 | tf_op jit(solution)/shard_map/reduce_scatter | solution.py:219
  212.4 7.5 %copy-start.2 = (f32[1152,4608]{1,0:T(8,128)}, f32[1152,4608]{1,0:T(8,128)S(1)}, u32[]{:S(2)}) copy-start(f32[1152,4608]{1,0:T(8,128)S(1)} %get-tuple-element.37) | copy-start | bytes 63700996
  289.8 2.3 slice-start.1
  289.8 3.5 copy-start.4
  293.3 3.1 slice-start
  301.8 40.1 %copy-start.5 = (bf16[1,2,32,384]{3,2,1,0:T(8,128)(2,1)S(1)}, bf16[1,2,32,384]{3,2,1,0:T(8,128)(2,1)}, u32[]{:S(2)}) copy-start(bf16[1,2,32,384]{3,2,1,0:T(8,128)(2,1)} %param.12) | copy-start | bytes 147460
  301.8 48.1 %copy-start.1 = (bf16[192,3,384]{2,0,1:T(8,128)(2,1)S(1)}, bf16[192,3,384]{2,0,1:T(8,128)(2,1)}, u32[]{:S(2)}) copy-start(bf16[192,3,384]{2,0,1:T(8,128)(2,1)} %param.15) | copy-start | bytes 1327108
  343.1 5.8 %collective-permute-start = (bf16[1,256,384]{2,1,0:T(8,128)(2,1)S(1)}, bf16[1,256,384]{2,1,0:T(8,128)(2,1)S(1)}, u32[]{:S(2)}, u32[]{:S(2)}) collective-permute-start(bf16[1,256,384]{2,1,0:T(8,128)(2,1)S(1)} %constant_dynamic-slice_fusion), channel_id=1, source_target_pairs={{0,128},{128,0},{1,129},{129,1},{2,130},{130,2},{3,131},{131,3},{4... | collective-permute-start | bytes 589832 | tf_op jit(solution)/shard_map/ppermute | solution.py:230
Sparse Core Ops, SparseCore 0:
  11.0 81.1 all-gather.2
  94.6 195.1 all-gather.4
  301.9 39.9 reduce-scatter.1
